TPU v7x, 256 devices: a whole 4x4x8 slice. The times are simulated.
256 devices in a mesh: island: 4 (over x_lo, core), fsdp: 64 (over x_hi, z, y).
Axes of the slice: x: 4 (x_hi: 2, x_lo: 2; x = x_hi * 2 + x_lo), y: 4, z: 8, core: 2. Of those that a mesh axis runs over, the one named last changes fastest.
Arguments:
- acts: bfloat16 [65536, 8192], P(('island', 'fsdp')), may hold values from -24 to 24
- cotangent: bfloat16 [65536, 512], P(('island', 'fsdp')), may hold values from -6 to 6
- global_params: float32 [8192, 512], P('fsdp'), may hold values from -0.12 to 0.12
- momentum: float32 [8192, 512], P('fsdp'), may hold values from -0.18 to 0.18
- island_drift: float32 [4, 8192, 512], P('island', 'fsdp'), may hold values from -0.12 to 0.12
- moment1: float32 [4, 8192, 512], P('island', 'fsdp'), may hold values from -6 to 6
- moment2: float32 [4, 8192, 512], P('island', 'fsdp'), may hold values from 0.05 to 1
Outputs:
- keys: bfloat16 [65536, 512], P(('island', 'fsdp'))
- new_global: float32 [8192, 512], P('fsdp')
- new_momentum: float32 [8192, 512], P('fsdp')
- moment1_out: float32 [4, 8192, 512], P('island', 'fsdp')
- moment2_out: float32 [4, 8192, 512], P('island', 'fsdp')
All inputs are finite; a program needn't handle non-finite values.
Results may differ from a plain program's by a relative error of at most 0.0049.
Values may be sent and summed in bfloat16 or wider, within the bound.
No kernel may reach another device: no remote copies, remote signals or barrier semaphores. Data moves between devices by JAX's collectives and lax.ppermute only.
A program may use at most 128 MiB of HBM per device.

v0:
```python
import jax
import jax.numpy as jnp
from jax import lax
from jax.sharding import Mesh, PartitionSpec as P

D = 8192
FS = ("xh", "z", "y")
beta_one = 0.9
beta_two = 0.95
epsilon = 1e-08
inner_rate = 0.05
decay_rate = 0.1
outer_rate = 0.7
nesterov = 0.9


def per_device(acts, cotangent, global_params, momentum, island_drift, moment1, moment2):
    fsdp_count = lax.axis_size(FS)
    island_count = lax.axis_size("island")
    scale = (acts.shape[0] * fsdp_count) ** (-0.5)
    xh_n, z_n, y_n = (lax.axis_size(a) for a in ("xh", "z", "y"))
    tokens = acts.shape[0]
    acts_perm = (
        acts.reshape(tokens, xh_n, z_n, D // (xh_n * z_n)).transpose(0, 2, 1, 3).reshape(tokens, D)
    )
    partial = lax.dot_general(
        acts_perm, cotangent, (((0,), (0,)), ((), ())), preferred_element_type=jnp.float32
    )
    grad = lax.psum_scatter(partial, "z", scatter_dimension=0, tiled=True)
    grad = lax.psum_scatter(grad, "xh", scatter_dimension=0, tiled=True)
    grad = lax.psum_scatter(grad, "y", scatter_dimension=0, tiled=True)
    grad = grad * scale
    drift = island_drift[0]
    first = beta_one * moment1[0] + (1.0 - beta_one) * grad
    second = beta_two * moment2[0] + (1.0 - beta_two) * grad * grad
    step = first / (jnp.sqrt(second) + epsilon) + decay_rate * (global_params - drift)
    pseudo = drift + inner_rate * step
    pair_core = [(i, i ^ 1) for i in range(island_count)]
    pair_chip = [(i, i ^ 2) for i in range(island_count)]
    summed = pseudo + lax.ppermute(pseudo, "island", pair_core)
    summed = summed + lax.ppermute(summed, "island", pair_chip)
    mean = summed / island_count
    new_momentum = nesterov * momentum + mean
    new_global = global_params - outer_rate * (mean + nesterov * new_momentum)
    weights = new_global.astype(jnp.bfloat16)
    core = lax.axis_index("island") % 2
    half = weights.shape[1] // 2
    own = lax.dynamic_slice_in_dim(weights, core * half, half, axis=1)
    own_full = lax.all_gather(own, FS, axis=0, tiled=True)
    other_full = lax.ppermute(own_full, "island", pair_core)
    keys_own = jnp.dot(acts, own_full, preferred_element_type=jnp.float32)
    keys_other = jnp.dot(acts, other_full, preferred_element_type=jnp.float32)
    keys_own = (keys_own * D ** (-0.5)).astype(jnp.bfloat16)
    keys_other = (keys_other * D ** (-0.5)).astype(jnp.bfloat16)
    is_first = core == 0
    keys = jnp.concatenate(
        [jnp.where(is_first, keys_own, keys_other), jnp.where(is_first, keys_other, keys_own)],
        axis=1,
    )
    return (keys, new_global, new_momentum, first[None], second[None])


def solution(mesh):
    fsdp_n = mesh.shape["fsdp"]
    mesh = Mesh(mesh.devices.reshape(mesh.shape["island"], 2, 8, fsdp_n // 16), ("island",) + FS)
    return jax.shard_map(
        per_device,
        mesh=mesh,
        in_specs=(
            P(("island", *FS), None),
            P(("island", *FS), None),
            P(FS, None),
            P(FS, None),
            P("island", FS, None),
            P("island", FS, None),
            P("island", FS, None),
        ),
        out_specs=(
            P(("island", *FS), None),
            P(FS, None),
            P(FS, None),
            P("island", FS, None),
            P("island", FS, None),
        ),
        check_vma=False,
    )
```

profile of v0, /device:TPU:1, one launch (start us, length us, event | category | flops | bytes accessed | tf_op | source)
XLA Modules:
  0.0 432.0 jit_solution(1409496534043252752)
XLA Ops:
  7.2 0.0 reduce-scatter.4.cloned.1.call-start
  7.2 6.4 %copy.14 = bf16[256,8192]{0,1:T(8,128)(2,1)} copy(bf16[256,8192]{1,0:T(8,128)(2,1)} %param.7) | data formatting | bytes 8388608 | tf_op args[0]
  13.6 2.5 copy.15
  16.1 8.1 %fusion.7 = f32[8192,512]{1,0:T(8,128)} fusion(bf16[256,8192]{0,1:T(8,128)(2,1)S(1)} %bitcast.42, bf16[256,512]{1,0:T(8,128)(2,1)S(1)} %copy-done), kind=kOutput, calls=%fused_computation.20 | convolution fusion | flops 2147483648 | bytes 21233664 | tf_op jit(solution)/shard_map/dot_general | solution.py:26
  24.2 0.0 reduce-scatter.4.cloned.1.call-update
  24.3 0.0 reduce-scatter.6.cloned.1.call-start
  24.3 177.4 %reduce-scatter.4.cloned.1.call-done = f32[1024,512]{1,0:T(8,128)} async-done(((f32[8192,512]{1,0:T(8,128)}), f32[1024,512]{1,0:T(8,128)}) %reduce-scatter.4.cloned.1.call-update) | async-done | bytes 2097168 | tf_op jit(solution)/shard_map/reduce_scatter | solution.py:29
  201.7 0.0 reduce-scatter.8.cloned.1.call-start
  201.8 39.5 %reduce-scatter.6.cloned.1.call-done = f32[512,512]{1,0:T(8,128)} async-done(((f32[1024,512]{1,0:T(8,128)}), f32[512,512]{1,0:T(8,128)}) %reduce-scatter.6.cloned.1.call-update) | async-done | bytes 1048592 | tf_op jit(solution)/shard_map/reduce_scatter | solution.py:30
  241.2 0.0 all-gather.2.cloned.1.call-start
  241.3 27.0 %reduce-scatter.8.cloned.1.call-done = f32[128,512]{1,0:T(8,128)} async-done(((f32[512,512]{1,0:T(8,128)}), f32[128,512]{1,0:T(8,128)}) %reduce-scatter.8.cloned.1.call-update) | async-done | bytes 262160 | tf_op jit(solution)/shard_map/reduce_scatter | solution.py:31
  268.3 1.9 fusion.6
  270.2 2.2 collective-permute-start
  272.4 1.2 collective-permute-done
  273.6 1.3 collective-permute-start.1
  274.9 6.3 %collective-permute-done.1 = f32[128,512]{1,0:T(8,128)S(1)} collective-permute-done((f32[128,512]{1,0:T(8,128)S(1)}, f32[128,512]{1,0:T(8,128)S(1)}, u32[]{:S(2)}, u32[]{:S(2)}) %collective-permute-start.1) | collective-permute-done | bytes 262176 | tf_op jit(solution)/shard_map/ppermute | solution.py:41
  281.2 0.8 multiply_subtract_fusion
  282.0 0.7 dynamic-slice_convert_fusion
  282.8 124.4 %all-gather.2.cloned.1.call-done = bf16[8192,256]{1,0:T(8,128)(2,1)} async-done(((bf16[128,256]{1,0:T(8,128)(2,1)}), bf16[8192,256]{1,0:T(8,128)(2,1)}) %all-gather.2.cloned.1.call-update) | async-done | bytes 4194320 | tf_op jit(solution)/shard_map/all_gather | solution.py:49
  407.1 4.2 collective-permute-start.2
  411.4 7.1 %collective-permute-done.2 = bf16[8192,256]{1,0:T(8,128)(2,1)} collective-permute-done((bf16[8192,256]{1,0:T(8,128)(2,1)}, bf16[8192,256]{1,0:T(8,128)(2,1)}, u32[]{:S(2)}, u32[]{:S(2)}) %collective-permute-start.2) | collective-permute-done | bytes 4194336 | tf_op jit(solution)/shard_map/ppermute | solution.py:50
  418.5 4.8 %fusion.1 = bf16[256,256]{1,0:T(8,128)(2,1)S(1)} fusion(bf16[8192,256]{1,0:T(8,128)(2,1)} %collective-permute-done.2, bf16[256,8192]{1,0:T(8,128)(2,1)} %param.7), kind=kOutput, calls=%fused_computation.3 | convolution fusion | flops 1073872896 | bytes 8519680 | tf_op jit(solution)/shard_map/dot_general | solution.py:52
  423.3 1.3 select_bitcast_fusion.1
  424.6 0.8 copy.16
  (23 shorter events, 0.2 us)
Async XLA Ops:
  7.2 8.9 %copy-start = (bf16[256,512]{1,0:T(8,128)(2,1)S(1)}, bf16[256,512]{1,0:T(8,128)(2,1)}, u32[]{:S(2)}) copy-start(bf16[256,512]{1,0:T(8,128)(2,1)} %param.8) | copy-start | bytes 786436
  7.2 194.5 %reduce-scatter.4.cloned.1.call-start = ((), (), s32[]{:S(2)}) async-start(), calls=%async_computation.3 | async-start | bytes 18874368 | tf_op jit(solution)/shard_map/reduce_scatter | solution.py:29
  24.2 244.1 %copy-start.2 = (f32[128,512]{1,0:T(8,128)S(1)}, f32[128,512]{1,0:T(8,128)}, u32[]{:S(2)}) copy-start(f32[128,512]{1,0:T(8,128)} %param.9) | copy-start | bytes 786436
  24.2 244.1 %copy-start.5 = (f32[1,128,512]{2,1,0:T(8,128)S(1)}, f32[1,128,512]{2,1,0:T(8,128)}, u32[]{:S(2)}) copy-start(f32[1,128,512]{2,1,0:T(8,128)} %param.13) | copy-start | bytes 786436
  24.2 244.1 %copy-start.6 = (f32[1,128,512]{2,1,0:T(8,128)S(1)}, f32[1,128,512]{2,1,0:T(8,128)}, u32[]{:S(2)}) copy-start(f32[1,128,512]{2,1,0:T(8,128)} %param.12) | copy-start | bytes 786436
  24.2 244.1 %copy-start.7 = (f32[1,128,512]{2,1,0:T(8,128)S(1)}, f32[1,128,512]{2,1,0:T(8,128)}, u32[]{:S(2)}) copy-start(f32[1,128,512]{2,1,0:T(8,128)} %param.11) | copy-start | bytes 786436
  24.2 257.0 %copy-start.4 = (f32[128,512]{1,0:T(8,128)S(1)}, f32[128,512]{1,0:T(8,128)}, u32[]{:S(2)}) copy-start(f32[128,512]{1,0:T(8,128)} %param.10) | copy-start | bytes 786436
  24.3 217.0 %reduce-scatter.6.cloned.1.call-start = ((), (), s32[]{:S(2)}) async-start(), calls=%async_computation.4 | async-start | bytes 3145728 | tf_op jit(solution)/shard_map/reduce_scatter | solution.py:30
  201.7 66.6 %reduce-scatter.8.cloned.1.call-start = ((), (), s32[]{:S(2)}) async-start(), calls=%async_computation.5 | async-start | bytes 1310720 | tf_op jit(solution)/shard_map/reduce_scatter | solution.py:31
  241.2 165.9 %all-gather.2.cloned.1.call-start = ((), (), s32[]{:S(2)}) async-start(), calls=%async_computation.6 | async-start | bytes 4259840 | tf_op jit(solution)/shard_map/all_gather | solution.py:49
  270.2 3.4 collective-permute-start
  273.6 7.6 %collective-permute-start.1 = (f32[128,512]{1,0:T(8,128)S(1)}, f32[128,512]{1,0:T(8,128)S(1)}, u32[]{:S(2)}, u32[]{:S(2)}) collective-permute-start(f32[128,512]{1,0:T(8,128)S(1)} %add.50), channel_id=1, source_target_pairs={{0,128},{64,192},{128,0},{192,64},{1,129},{65,193},{129,1},{193,65... | collective-permute-start | bytes 786440 | tf_op jit(solution)/shard_map/ppermute | solution.py:41
  282.0 141.2 %copy-start.3 = (f32[128,512]{1,0:T(8,128)}, f32[128,512]{1,0:T(8,128)S(1)}, u32[]{:S(2)}) copy-start(f32[128,512]{1,0:T(8,128)S(1)} %get-tuple-element.20) | copy-start | bytes 786436
  407.1 11.4 %collective-permute-start.2 = (bf16[8192,256]{1,0:T(8,128)(2,1)}, bf16[8192,256]{1,0:T(8,128)(2,1)}, u32[]{:S(2)}, u32[]{:S(2)}) collective-permute-start(bf16[8192,256]{1,0:T(8,128)(2,1)} %all-gather.2.cloned.1.call-done), channel_id=1, source_target_pairs={{0,64},{64,0},{128,192},{192,128},{1,65},{65,1},{129,193},{193,129... | collective-permute-start | bytes 12582920 | tf_op jit(solution)/shard_map/ppermute | solution.py:50
  411.3 11.9 %copy-start.1 = (bf16[256,8192]{1,0:T(8,128)(2,1)S(1)}, bf16[256,8192]{1,0:T(8,128)(2,1)}, u32[]{:S(2)}) copy-start(bf16[256,8192]{1,0:T(8,128)(2,1)} %param.7) | copy-start | bytes 12582916
  411.3 11.9 %copy-start.8 = (bf16[8192,256]{1,0:T(8,128)(2,1)S(1)}, bf16[8192,256]{1,0:T(8,128)(2,1)}, u32[]{:S(2)}) copy-start(bf16[8192,256]{1,0:T(8,128)(2,1)} %all-gather.2.cloned.1.call-done) | copy-start | bytes 12582916
Sparse Core Ops, SparseCore 0:
  24.4 177.2 reduce-scatter.3
  204.2 36.9 reduce-scatter.5
  243.8 24.4 reduce-scatter.7
  282.9 124.1 all-gather.1
where the time goes:
time: 432 us
  waiting for transfers between devices  383 us (89%)
  matrix products  14.2 us (3%)
  between operations  13.9 us (3%)
  local copies, waits for them, and re-layouts  10.4 us (2%)
  starting transfers between devices  7.87 us (2%)
    reduce_scatter x1, waiting for transfers between devices, per_device(): grad = lax.psum_scatter(partial, 'z', scatter_dimension=0, tiled=True)  177 us
    all_gather x1, waiting for transfers between devices, per_device(): own_full = lax.all_gather(own, FS, axis=0, tiled=True)  124 us
    reduce_scatter x1, waiting for transfers between devices, per_device(): grad = lax.psum_scatter(grad, 'xh', scatter_dimension=0, tiled=True)  39.5 us
    reduce_scatter x1, waiting for transfers between devices, per_device(): grad = lax.psum_scatter(grad, 'y', scatter_dimension=0, tiled=True)  27 us
  transfers between devices with their start and end apart: 7, of which 7 were waited for; matrix products, arithmetic and copies ran while one was open for 0% of the time, Pallas kernels for 0%

commit v1 on v0

--- a/solution.py
+++ b/solution.py
@@ -46,7 +46,11 @@
     core = lax.axis_index("island") % 2
     half = weights.shape[1] // 2
     own = lax.dynamic_slice_in_dim(weights, core * half, half, axis=1)
-    own_full = lax.all_gather(own, FS, axis=0, tiled=True)
+    work_group = lambda base_x: jnp.concatenate(
+        jax.lax.all_to_all(jnp.stack([base_x for _ in range(jax.lax.axis_size(FS))]), FS, 0, 0),
+        axis=0,
+    )
+    own_full = work_group(own)
     other_full = lax.ppermute(own_full, "island", pair_core)
     keys_own = jnp.dot(acts, own_full, preferred_element_type=jnp.float32)
     keys_other = jnp.dot(acts, other_full, preferred_element_type=jnp.float32)

time: 432 us -> 410 us (0.949)
  waiting for transfers between devices: 383 us -> 254 us
  blocking collectives: 0 us -> 105 us
    all_gather x1 -> x0, waiting for transfers between devices: 124 us -> none  [per_device(): own_full = lax.all_gather(own, FS, axis=0, tiled=True)]
    all_to_all x0 -> x1, blocking collectives: none -> 105 us  [per_device(): jax.lax.all_to_all(jnp.stack([base_x for _ in range(jax.lax.axis_size(FS)...]
    ppermute x1, waiting for transfers between devices: 7.12 us -> 2.22 us  [per_device(): other_full = lax.ppermute(own_full, 'island', pair_core)]
  transfers between devices with their start and end apart: 7 -> 6, of which waited for: 7 -> 6; matrix products, arithmetic and copies ran while one was open for 0% -> 1% of each run, Pallas kernels for 0% -> 0%
where the time goes in v1:
time: 410 us; the launch traced here: 409 us
  waiting for transfers between devices  254 us (62%)
  blocking collectives  105 us (26%)
  matrix products  16.5 us (4%)
  between operations  13.8 us (3%)
  local copies, waits for them, and re-layouts  10.3 us (3%)
  starting transfers between devices  7.4 us (2%)
    reduce_scatter x1, waiting for transfers between devices, per_device(): grad = lax.psum_scatter(partial, 'z', scatter_dimension=0, tiled=True)  177 us
    all_to_all x1, blocking collectives, per_device(): jax.lax.all_to_all(jnp.stack([base_x for _ in range(jax.lax.axis_size(FS)...  105 us
    reduce_scatter x1, waiting for transfers between devices, per_device(): grad = lax.psum_scatter(grad, 'xh', scatter_dimension=0, tiled=True)  39.5 us
    reduce_scatter x1, waiting for transfers between devices, per_device(): grad = lax.psum_scatter(grad, 'y', scatter_dimension=0, tiled=True)  27 us
  transfers between devices with their start and end apart: 6, of which 6 were waited for; matrix products, arithmetic and copies ran while one was open for 1% of the time, Pallas kernels for 0%

profile of v1, /device:TPU:1, one launch (start us, length us, event | category | flops | bytes accessed | tf_op | source)
XLA Modules:
  0.0 409.1 jit_solution(15761667640762347669)
XLA Ops:
  7.2 0.0 reduce-scatter.4.cloned.1.call-start
  7.2 6.4 %copy.14 = bf16[256,8192]{0,1:T(8,128)(2,1)} copy(bf16[256,8192]{1,0:T(8,128)(2,1)} %param.7) | data formatting | bytes 8388608 | tf_op args[0]
  13.6 2.5 copy.15
  16.1 8.1 %fusion.7 = f32[8192,512]{1,0:T(8,128)} fusion(bf16[256,8192]{0,1:T(8,128)(2,1)S(1)} %bitcast.43, bf16[256,512]{1,0:T(8,128)(2,1)S(1)} %copy-done), kind=kOutput, calls=%fused_computation.20 | convolution fusion | flops 2147483648 | bytes 21233664 | tf_op jit(solution)/shard_map/dot_general | solution.py:26
  24.2 0.0 reduce-scatter.4.cloned.1.call-update
  24.2 0.0 reduce-scatter.6.cloned.1.call-start
  24.3 177.4 %reduce-scatter.4.cloned.1.call-done = f32[1024,512]{1,0:T(8,128)} async-done(((f32[8192,512]{1,0:T(8,128)}), f32[1024,512]{1,0:T(8,128)}) %reduce-scatter.4.cloned.1.call-update) | async-done | bytes 2097168 | tf_op jit(solution)/shard_map/reduce_scatter | solution.py:29
  201.7 0.0 reduce-scatter.8.cloned.1.call-start
  201.8 39.5 %reduce-scatter.6.cloned.1.call-done = f32[512,512]{1,0:T(8,128)} async-done(((f32[1024,512]{1,0:T(8,128)}), f32[512,512]{1,0:T(8,128)}) %reduce-scatter.6.cloned.1.call-update) | async-done | bytes 1048592 | tf_op jit(solution)/shard_map/reduce_scatter | solution.py:30
  241.2 0.0 reduce-scatter.8.cloned.1.call-update
  241.2 27.0 %reduce-scatter.8.cloned.1.call-done = f32[128,512]{1,0:T(8,128)} async-done(((f32[512,512]{1,0:T(8,128)}), f32[128,512]{1,0:T(8,128)}) %reduce-scatter.8.cloned.1.call-update) | async-done | bytes 262160 | tf_op jit(solution)/shard_map/reduce_scatter | solution.py:31
  268.3 1.9 fusion.6
  270.2 2.2 collective-permute-start
  272.4 1.2 collective-permute-done
  273.6 1.2 collective-permute-start.1
  274.8 6.4 %collective-permute-done.1 = f32[128,512]{1,0:T(8,128)S(1)} collective-permute-done((f32[128,512]{1,0:T(8,128)S(1)}, f32[128,512]{1,0:T(8,128)S(1)}, u32[]{:S(2)}, u32[]{:S(2)}) %collective-permute-start.1) | collective-permute-done | bytes 262176 | tf_op jit(solution)/shard_map/ppermute | solution.py:41
  281.2 0.8 multiply_subtract_fusion
  282.0 0.5 stack.2
  282.5 104.7 %all_to_all.5 = bf16[64,128,256]{2,1,0:T(8,128)(2,1)} all-to-all(bf16[64,128,256]{2,1,0:T(8,128)(2,1)S(1)} %stack.2), channel_id=1, replica_groups=mesh['island'=4,'xh'=2,'z'=8,'y'=4] {'xh','z','y'}, dimensions={0} | all-to-all | bytes 8388608 | tf_op jit(solution)/shard_map/all_to_all | solution.py:50
  387.2 3.9 collective-permute-start.2
  391.1 4.9 %fusion = bf16[256,256]{1,0:T(8,128)(2,1)S(1)} fusion(bf16[8192,256]{1,0:T(8,128)(2,1)} %bitcast.6, bf16[256,8192]{1,0:T(8,128)(2,1)} %param.7), kind=kOutput, calls=%fused_computation.2 | convolution fusion | flops 1073872896 | bytes 8519680 | tf_op jit(solution)/shard_map/dot_general | solution.py:55
  396.0 2.2 collective-permute-done.2
  398.2 3.5 select_bitcast_fusion.1
  401.7 0.8 copy.16
  (20 shorter events, 0.1 us)
Async XLA Ops:
  7.2 8.9 %copy-start = (bf16[256,512]{1,0:T(8,128)(2,1)S(1)}, bf16[256,512]{1,0:T(8,128)(2,1)}, u32[]{:S(2)}) copy-start(bf16[256,512]{1,0:T(8,128)(2,1)} %param.8) | copy-start | bytes 786436
  7.2 194.5 %reduce-scatter.4.cloned.1.call-start = ((), (), s32[]{:S(2)}) async-start(), calls=%async_computation.4 | async-start | bytes 18874368 | tf_op jit(solution)/shard_map/reduce_scatter | solution.py:29
  24.2 244.1 %copy-start.2 = (f32[128,512]{1,0:T(8,128)S(1)}, f32[128,512]{1,0:T(8,128)}, u32[]{:S(2)}) copy-start(f32[128,512]{1,0:T(8,128)} %param.9) | copy-start | bytes 786436
  24.2 244.1 %copy-start.5 = (f32[1,128,512]{2,1,0:T(8,128)S(1)}, f32[1,128,512]{2,1,0:T(8,128)}, u32[]{:S(2)}) copy-start(f32[1,128,512]{2,1,0:T(8,128)} %param.13) | copy-start | bytes 786436
  24.2 244.1 %copy-start.6 = (f32[1,128,512]{2,1,0:T(8,128)S(1)}, f32[1,128,512]{2,1,0:T(8,128)}, u32[]{:S(2)}) copy-start(f32[1,128,512]{2,1,0:T(8,128)} %param.12) | copy-start | bytes 786436
  24.2 244.1 %copy-start.7 = (f32[1,128,512]{2,1,0:T(8,128)S(1)}, f32[1,128,512]{2,1,0:T(8,128)}, u32[]{:S(2)}) copy-start(f32[1,128,512]{2,1,0:T(8,128)} %param.11) | copy-start | bytes 786436
  24.2 257.0 %copy-start.4 = (f32[128,512]{1,0:T(8,128)S(1)}, f32[128,512]{1,0:T(8,128)}, u32[]{:S(2)}) copy-start(f32[128,512]{1,0:T(8,128)} %param.10) | copy-start | bytes 786436
  24.2 217.0 %reduce-scatter.6.cloned.1.call-start = ((), (), s32[]{:S(2)}) async-start(), calls=%async_computation.5 | async-start | bytes 3145728 | tf_op jit(solution)/shard_map/reduce_scatter | solution.py:30
  201.7 66.6 %reduce-scatter.8.cloned.1.call-start = ((), (), s32[]{:S(2)}) async-start(), calls=%async_computation.6 | async-start | bytes 1310720 | tf_op jit(solution)/shard_map/reduce_scatter | solution.py:31
  270.2 3.4 collective-permute-start
  273.6 7.6 %collective-permute-start.1 = (f32[128,512]{1,0:T(8,128)S(1)}, f32[128,512]{1,0:T(8,128)S(1)}, u32[]{:S(2)}, u32[]{:S(2)}) collective-permute-start(f32[128,512]{1,0:T(8,128)S(1)} %add.50), channel_id=1, source_target_pairs={{0,128},{64,192},{128,0},{192,64},{1,129},{65,193},{129,1},{193,65... | collective-permute-start | bytes 786440 | tf_op jit(solution)/shard_map/ppermute | solution.py:41
  282.0 105.2 %copy-start.3 = (f32[128,512]{1,0:T(8,128)}, f32[128,512]{1,0:T(8,128)S(1)}, u32[]{:S(2)}) copy-start(f32[128,512]{1,0:T(8,128)S(1)} %get-tuple-element.20) | copy-start | bytes 786436
  387.2 11.0 %collective-permute-start.2 = (bf16[8192,256]{1,0:T(8,128)(2,1)}, bf16[8192,256]{1,0:T(8,128)(2,1)}, u32[]{:S(2)}, u32[]{:S(2)}) collective-permute-start(bf16[8192,256]{1,0:T(8,128)(2,1)} %bitcast.6), channel_id=1, source_target_pairs={{0,64},{64,0},{128,192},{192,128},{1,65},{65,1},{129,193},{193,129... | collective-permute-start | bytes 12582920 | tf_op jit(solution)/shard_map/ppermute | solution.py:54
  391.1 7.1 %copy-start.1 = (bf16[256,8192]{1,0:T(8,128)(2,1)S(1)}, bf16[256,8192]{1,0:T(8,128)(2,1)}, u32[]{:S(2)}) copy-start(bf16[256,8192]{1,0:T(8,128)(2,1)} %param.7) | copy-start | bytes 12582916
Sparse Core Ops, SparseCore 0:
  24.4 177.2 reduce-scatter.3
  204.2 36.9 reduce-scatter.5
  243.8 24.4 reduce-scatter.7
